TPU v7x, 512 devices: a whole 4x8x8 slice. The times are simulated.
512 devices in a mesh: dp: 32 (over z, x), fsdp: 16 (over y, core).
Axes of the slice: x: 4, y: 8, z: 8, core: 2. Of those that a mesh axis runs over, the one named last changes fastest.
Arguments:
- projected: bfloat16 [65536, 2304], P(('dp', 'fsdp')), may hold values from -7.03125 to 7.03125
- out_weight: bfloat16 [768, 1536], P('fsdp'), may hold values from -0.21875 to 0.21875
- kernel: float32 [31, 1536], replicated, may hold values from -2 to 2
- cotangent: bfloat16 [65536, 1536], P(('dp', 'fsdp')), may hold values from -6 to 6
- send_rows: int32 [65536], P(('dp', 'fsdp')), may hold values from -1 to 127, as said below
- compute_src: int32 [65536], P(('dp', 'fsdp')), may hold values from -1 to 127, as said below
- segment: int32 [65536], P(('dp', 'fsdp')), may hold values from -1 to 3, as said below
Outputs:
- block_out: bfloat16 [65536, 1536], P(('dp', 'fsdp'))
- projected_grad: bfloat16 [65536, 2304], P(('dp', 'fsdp'))
- out_weight_grad: float32 [768, 1536], P('fsdp')
- kernel_grad: float32 [31, 1536], replicated
Inputs may be any that keep to these rules, and one draw needn't show every extreme that they name: `send_rows`: A device's 128 entries are 32 blocks of 4, block t for index t of dp at the same fsdp index; each lists rows of the device's own block of projected, each row at most once, filled entries first in a block and -1 after them. In every draw some device of each fsdp index fills all its entries. `compute_src`: on device (t, f), a row holds s * 4 + k when it receives entry t * 4 + k of device (s, f); every filled entry of send_rows is received by exactly one row, and a row holds -1 when it receives nothing. Filled rows come first. In every draw some device of each fsdp index receives a full block from every device. On each device, rows with compute_src = -1 hold -1, the others hold segment numbers from 0 that never fall along the rows.
All inputs are finite; a program needn't handle non-finite values.
Results may differ from a plain program's by a relative error of at most 0.018.
Values may be sent and summed in bfloat16 or wider, within the bound.
No kernel may reach another device: no remote copies, remote signals or barrier semaphores. Data moves between devices by JAX's collectives and lax.ppermute only.
A program may use at most 128 MiB of HBM per device.

v0:
```python
import jax
import jax.numpy as jnp
from jax import lax
from jax.sharding import PartitionSpec as P

HEADS = 8
HEAD_DIM = 96


def split_heads(frames):
    length = frames.shape[0]
    inner_width = HEADS * HEAD_DIM
    query_part = frames[:, :inner_width].reshape(length, HEADS, HEAD_DIM)
    key_part = frames[:, inner_width : 2 * inner_width].reshape(length, HEADS, HEAD_DIM)
    value_part = frames[:, 2 * inner_width :].reshape(length, HEADS, HEAD_DIM)
    return (query_part, key_part, value_part)


def attend(frames, segment):
    query_part, key_part, value_part = split_heads(frames)
    scores = jnp.einsum(
        "qhd,khd->hqk", query_part, key_part, preferred_element_type=jnp.float32
    ) * HEAD_DIM ** (-0.5)
    inside = segment[:, None] == segment[None, :]
    scores = jnp.where(inside[None], scores, -1e30)
    highest = jnp.max(scores, axis=2, keepdims=True)
    weights = jnp.exp(scores - highest)
    soft_probs = weights / jnp.sum(weights, axis=2, keepdims=True)
    rounded = soft_probs.astype(jnp.bfloat16)
    context = jnp.einsum("hqk,khd->qhd", rounded, value_part, preferred_element_type=jnp.float32)
    return (
        context.reshape(frames.shape[0], HEADS * HEAD_DIM).astype(jnp.bfloat16),
        soft_probs,
        rounded,
    )


def attend_back(frames, soft_probs, rounded, context_grad):
    query_part, key_part, value_part = split_heads(frames)
    length = frames.shape[0]
    inner_width = HEADS * HEAD_DIM
    upstream = context_grad.reshape(length, HEADS, HEAD_DIM)
    value_grad = jnp.einsum("hqk,qhd->khd", rounded, upstream, preferred_element_type=jnp.float32)
    prob_grad = jnp.einsum("qhd,khd->hqk", upstream, value_part, preferred_element_type=jnp.float32)
    score_grad = soft_probs * (prob_grad - jnp.sum(prob_grad * soft_probs, axis=2, keepdims=True))
    score_grad = (score_grad * HEAD_DIM ** (-0.5)).astype(jnp.bfloat16)
    query_grad = jnp.einsum(
        "hqk,khd->qhd", score_grad, key_part, preferred_element_type=jnp.float32
    )
    key_grad = jnp.einsum(
        "hqk,qhd->khd", score_grad, query_part, preferred_element_type=jnp.float32
    )
    return jnp.concatenate(
        [
            query_grad.reshape(length, inner_width).astype(jnp.bfloat16),
            key_grad.reshape(length, inner_width).astype(jnp.bfloat16),
            value_grad.reshape(length, inner_width).astype(jnp.bfloat16),
        ],
        axis=1,
    )


def finish(mixed, kernel, segment):
    length = mixed.shape[0]
    tap_count = kernel.shape[0]
    half_span = (tap_count - 1) // 2
    signal = mixed.astype(jnp.float32)
    padded = jnp.pad(signal, ((half_span, half_span), (0, 0)))
    neighbours = jnp.pad(segment, (half_span, half_span), constant_values=-2)
    convolved = jnp.zeros_like(signal)
    for offset in range(tap_count):
        matching = (neighbours[offset : offset + length] == segment).astype(jnp.float32)
        convolved = (
            convolved + kernel[offset] * padded[offset : offset + length] * matching[:, None]
        )
    return signal + jax.nn.silu(convolved)


def body(projected, out_weight, kernel, cotangent, send_rows, compute_src, segment):
    row_count = projected.shape[0]
    present = send_rows >= 0
    outgoing = jnp.take(projected, jnp.maximum(send_rows, 0), axis=0)
    outgoing = jnp.where(present[:, None], outgoing, jnp.zeros_like(outgoing))
    incoming = lax.all_to_all(outgoing, "dp", split_axis=0, concat_axis=0, tiled=True)
    filled = compute_src >= 0
    frames = jnp.take(incoming, jnp.maximum(compute_src, 0), axis=0)
    frames = jnp.where(filled[:, None], frames, jnp.zeros_like(frames))
    context, soft_probs, rounded = attend(frames, segment)
    columns = context
    mixed_sums = jnp.dot(
        columns,
        lax.all_gather(out_weight, "fsdp", axis=0, tiled=True),
        preferred_element_type=jnp.float32,
    )
    mixed = mixed_sums.astype(jnp.bfloat16)
    result, pullback = jax.vjp(
        lambda signal, kernel_taps: finish(signal, kernel_taps, segment), mixed, kernel
    )
    mixed_grad, kernel_part = pullback(cotangent.astype(jnp.float32))
    columns = context
    weight_share = lax.psum_scatter(
        jnp.einsum("rc,rd->cd", columns, mixed_grad, preferred_element_type=jnp.float32).astype(
            jnp.bfloat16
        ),
        "fsdp",
        scatter_dimension=0,
        tiled=True,
    ).astype(jnp.float32)
    context_grad = jnp.einsum(
        "rd,cd->rc",
        mixed_grad,
        lax.all_gather(out_weight, "fsdp", axis=0, tiled=True),
        preferred_element_type=jnp.float32,
    ).astype(jnp.bfloat16)
    frame_grad = attend_back(frames, soft_probs, rounded, context_grad)
    slot_total = incoming.shape[0]
    back_index = jnp.where(filled, compute_src, slot_total)
    returning = jnp.zeros_like(incoming).at[back_index].set(frame_grad, mode="drop")
    arrived = lax.all_to_all(returning, "dp", split_axis=0, concat_axis=0, tiled=True)
    source_index = jnp.where(present, send_rows, row_count)
    projected_grad = jnp.zeros_like(projected).at[source_index].set(arrived, mode="drop")
    scale_factor = (row_count * lax.axis_size("dp") * lax.axis_size("fsdp")) ** (-0.5)
    kernel_f = lax.psum(kernel_part, "fsdp")
    both = dp_allreduce_a2a(
        jnp.concatenate([weight_share, kernel_f, jnp.zeros((17, 1536), jnp.float32)], axis=0)
    )
    weight_total, kernel_total = (both[:48], both[48:79])
    return (
        result.astype(jnp.bfloat16),
        projected_grad,
        weight_total * scale_factor,
        kernel_total * scale_factor,
    )


def dp_allreduce_rs_ag(x):
    n = lax.axis_size("dp")
    flat = x.reshape(n, -1)
    part = lax.psum_scatter(flat, "dp", scatter_dimension=0, tiled=True)
    return lax.all_gather(part, "dp", axis=0, tiled=True).reshape(x.shape)


def dp_allreduce_a2a(x):
    n = lax.axis_size("dp")
    flat = x.reshape(n, -1)
    got = lax.all_to_all(flat, "dp", split_axis=0, concat_axis=0, tiled=True)
    part = jnp.sum(got, axis=0, keepdims=True)
    return lax.all_gather(part, "dp", axis=0, tiled=True).reshape(x.shape)


def dp_allreduce_a2a2(x):
    n = lax.axis_size("dp")
    flat = x.reshape(n, -1)
    got = lax.all_to_all(flat, "dp", split_axis=0, concat_axis=0, tiled=True)
    part = jnp.sum(got, axis=0, keepdims=True)
    back = lax.all_to_all(
        jnp.broadcast_to(part, flat.shape), "dp", split_axis=0, concat_axis=0, tiled=True
    )
    return back.reshape(x.shape)


def solution(mesh):
    placed = (
        P(("dp", "fsdp"), None),
        P("fsdp", None),
        P(),
        P(("dp", "fsdp"), None),
        P(("dp", "fsdp")),
        P(("dp", "fsdp")),
        P(("dp", "fsdp")),
    )
    return jax.shard_map(
        body,
        mesh=mesh,
        in_specs=placed,
        out_specs=(P(("dp", "fsdp"), None), P(("dp", "fsdp"), None), P("fsdp", None), P()),
        check_vma=False,
    )
```

profile of v0, /device:TPU:24, one launch (start us, length us, event | category | flops | bytes accessed | tf_op | source)
XLA Modules:
  0.0 341.6 jit_solution(10079741374050329405)
XLA Ops:
  7.9 1.2 compare_select_fusion.1
  9.1 1.0 gather_fusion
  10.3 1.0 all_to_all.22
  11.3 13.2 %all-to-all-start = ((bf16[32,4,2304]{2,1,0:T(4,128)(2,1)}), bf16[32,4,2304]{2,1,0:T(4,128)(2,1)S(1)}, u32[]{:S(2)}, u32[]{:S(2)}) async-start(bf16[32,4,2304]{2,1,0:T(4,128)(2,1)} %all_to_all.22), calls=%async_computation | async-start | bytes 1179648 | tf_op jit(solution)/shard_map/all_to_all | solution.py:84
  26.0 17.5 %all-to-all-done = bf16[32,4,2304]{2,1,0:T(4,128)(2,1)S(1)} async-done(((bf16[32,4,2304]{2,1,0:T(4,128)(2,1)}), bf16[32,4,2304]{2,1,0:T(4,128)(2,1)S(1)}, u32[]{:S(2)}, u32[]{:S(2)}) %all-to-all-start) | async-done | bytes 589856 | tf_op jit(solution)/shard_map/all_to_all | solution.py:84
  43.6 1.0 gather_fusion.1
  45.3 1.2 fusion.40
  47.0 9.4 %all-gather.4.cloned.1.call-done = bf16[768,1536]{1,0:T(8,128)(2,1)} async-done(((bf16[48,1536]{1,0:T(8,128)(2,1)}), bf16[768,1536]{1,0:T(8,128)(2,1)}) %all-gather.4.cloned.1.call-update) | async-done | bytes 2359312 | tf_op jit(solution)/shard_map/all_gather | solution.py:92
  56.4 2.2 fusion.2
  58.6 7.6 %multiply_reduce_fusion.31 = (f32[1536]{0:T(1024)}, f32[1536]{0:T(1024)}, f32[1536]{0:T(1024)}, f32[1536]{0:T(1024)}, f32[1536]{0:T(1024)}, /*index=5*/f32[1536]...) fusion(f32[128,1536]{1,0:T(8,128)S(1)} %fusion.2, ...), kind=kLoop, calls=%fused_computation.99 | loop fusion | flops 25152000 | bytes 3013632 | tf_op jit(solution)/shard_map/transpose(jvp())/reduce_sum | solution.py:74
  66.2 2.3 multiply_reduce_fusion.16
  70.5 2.6 multiply_reduce_fusion.4
  73.1 2.8 pad_add_fusion
  76.7 2.1 convolution_convert_fusion
  84.2 2.5 convolution_convert_fusion.5
  87.0 1.3 convolution_convert_fusion.2
  88.7 1.7 convolution_convert_fusion.3
  90.6 2.3 convolution_convert_fusion.4
  92.8 1.1 copy.42
  93.9 1.8 scatter_custom_fusion
  95.8 1.0 all_to_all.25
  96.8 10.3 %all-to-all-start.1 = ((bf16[32,4,2304]{2,1,0:T(4,128)(2,1)}), bf16[32,4,2304]{2,1,0:T(4,128)(2,1)S(1)}, u32[]{:S(2)}, u32[]{:S(2)}) async-start(bf16[32,4,2304]{2,1,0:T(4,128)(2,1)} %all_to_all.25), calls=%async_computation.1 | async-start | bytes 1179648 | tf_op jit(solution)/shard_map/all_to_all | solution.py:119
  107.2 2.4 multiply_reduce_fusion.22
  110.1 1.0 pad_add_fusion.7
  111.2 26.3 %reduce-scatter.2.cloned.1.call-done = bf16[48,1536]{1,0:T(8,128)(2,1)} async-done(((bf16[768,1536]{1,0:T(8,128)(2,1)}), bf16[48,1536]{1,0:T(8,128)(2,1)}) %reduce-scatter.2.cloned.1.call-update) | async-done | bytes 147472 | tf_op jit(solution)/shard_map/reduce_scatter | solution.py:101
  138.4 112.9 %all-reduce.66.cloned.1.call-done = f32[31,1536]{1,0:T(8,128)} async-done(((f32[31,1536]{1,0:T(8,128)}), f32[31,1536]{1,0:T(8,128)}) %all-reduce.66.cloned.1.call-update) | async-done | bytes 190480 | tf_op jit(solution)/shard_map/psum | solution.py:123
  251.3 1.0 maximum_maximum_fusion
  252.3 1.5 all_to_all.30
  253.8 10.2 %all-to-all-start.2 = ((f32[32,1,4608]{2,1,0:T(1,128)}), f32[32,1,4608]{2,1,0:T(1,128)S(1)}, u32[]{:S(2)}, u32[]{:S(2)}) async-start(f32[32,1,4608]{2,1,0:T(1,128)} %all_to_all.30), calls=%async_computation.3 | async-start | bytes 1179648 | tf_op jit(solution)/shard_map/all_to_all | solution.py:146
  264.2 2.4 scatter_custom_fusion.1
  266.6 17.0 %all-to-all-done.2 = f32[32,1,4608]{2,1,0:T(1,128)S(1)} async-done(((f32[32,1,4608]{2,1,0:T(1,128)}), f32[32,1,4608]{2,1,0:T(1,128)S(1)}, u32[]{:S(2)}, u32[]{:S(2)}) %all-to-all-start.2) | async-done | bytes 589856 | tf_op jit(solution)/shard_map/all_to_all | solution.py:146
  283.9 48.8 %all-gather.1 = f32[32,1,4608]{2,1,0:T(1,128)S(1)} all-gather(f32[1,1,4608]{2,1,0:T(1,128)S(1)} %reshape.348), channel_id=2, replica_groups=mesh['dp'=32,'fsdp'=16] {'dp'}, dimensions={0}, use_global_device_ids=true | all-gather | bytes 608256 | tf_op jit(solution)/shard_map/all_gather | solution.py:148
  (176 shorter events, 16.5 us)
Async XLA Ops:
  7.2 49.2 %all-gather.4.cloned.1.call-start = ((), (), s32[]{:S(2)}) async-start(), calls=%async_computation.4 | async-start | bytes 2506752 | tf_op jit(solution)/shard_map/all_gather | solution.py:92
  10.1 14.4 %copy-start.6 = (f32[31,1536]{1,0:T(8,128)S(1)}, f32[31,1536]{1,0:T(8,128)}, u32[]{:S(2)}) copy-start(f32[31,1536]{1,0:T(8,128)} %param.11) | copy-start | bytes 571396
  10.1 14.6 %copy-start.48 = (s32[128]{0:T(128)S(1)}, s32[128]{0:T(128)}, u32[]{:S(2)}) copy-start(s32[128]{0:T(128)} %param.14) | copy-start | bytes 1540
  10.1 15.5 %copy-start.46 = (s32[128]{0:T(128)S(1)}, s32[128]{0:T(128)}, u32[]{:S(2)}) copy-start(s32[128]{0:T(128)} %param.15) | copy-start | bytes 1540
  11.3 32.2 %all-to-all-start = ((bf16[32,4,2304]{2,1,0:T(4,128)(2,1)}), bf16[32,4,2304]{2,1,0:T(4,128)(2,1)S(1)}, u32[]{:S(2)}, u32[]{:S(2)}) async-start(bf16[32,4,2304]{2,1,0:T(4,128)(2,1)} %all_to_all.22), calls=%async_computation | async-start | bytes 1179648 | tf_op jit(solution)/shard_map/all_to_all | solution.py:84
  24.4 113.0 %reduce-scatter.2.cloned.1.call-start = ((), (), s32[]{:S(2)}) async-start(), calls=%async_computation.5 | async-start | bytes 2506752 | tf_op jit(solution)/shard_map/reduce_scatter | solution.py:101
  25.8 43.2 %copy-start.43 = (f32[128]{0:T(128)}, f32[128]{0:T(128)S(1)}, u32[]{:S(2)}) copy-start(f32[128]{0:T(128)S(1)} %get-tuple-element.120) | copy-start | bytes 1540
  25.8 43.2 %copy-start.44 = (f32[128]{0:T(128)}, f32[128]{0:T(128)S(1)}, u32[]{:S(2)}) copy-start(f32[128]{0:T(128)S(1)} %get-tuple-element.121) | copy-start | bytes 1540
  25.8 43.2 %copy-start.45 = (f32[128]{0:T(128)}, f32[128]{0:T(128)S(1)}, u32[]{:S(2)}) copy-start(f32[128]{0:T(128)S(1)} %get-tuple-element.122) | copy-start | bytes 1540
  25.8 43.9 %copy-start.37 = (f32[128]{0:T(128)}, f32[128]{0:T(128)S(1)}, u32[]{:S(2)}) copy-start(f32[128]{0:T(128)S(1)} %get-tuple-element.114) | copy-start | bytes 1540
  25.8 43.9 %copy-start.38 = (f32[128]{0:T(128)}, f32[128]{0:T(128)S(1)}, u32[]{:S(2)}) copy-start(f32[128]{0:T(128)S(1)} %get-tuple-element.115) | copy-start | bytes 1540
  25.8 43.9 %copy-start.39 = (f32[128]{0:T(128)}, f32[128]{0:T(128)S(1)}, u32[]{:S(2)}) copy-start(f32[128]{0:T(128)S(1)} %get-tuple-element.116) | copy-start | bytes 1540
  25.9 43.9 %copy-start.40 = (f32[128]{0:T(128)}, f32[128]{0:T(128)S(1)}, u32[]{:S(2)}) copy-start(f32[128]{0:T(128)S(1)} %get-tuple-element.117) | copy-start | bytes 1540
  25.9 43.9 %copy-start.41 = (f32[128]{0:T(128)}, f32[128]{0:T(128)S(1)}, u32[]{:S(2)}) copy-start(f32[128]{0:T(128)S(1)} %get-tuple-element.118) | copy-start | bytes 1540
  25.9 43.9 %copy-start.42 = (f32[128]{0:T(128)}, f32[128]{0:T(128)S(1)}, u32[]{:S(2)}) copy-start(f32[128]{0:T(128)S(1)} %get-tuple-element.119) | copy-start | bytes 1540
  26.0 20.5 %copy-start.36 = (pred[128,128]{0,1:T(8,128)(4,1)}, pred[128,128]{0,1:T(8,128)(4,1)S(1)}, u32[]{:S(2)}) copy-start(pred[128,128]{0,1:T(8,128)(4,1)S(1)} %broadcast_compare_fusion) | copy-start | bytes 49156
  44.9 42.0 %copy-start.2 = (bf16[128,768]{0,1:T(8,128)(2,1)}, bf16[128,768]{0,1:T(8,128)(2,1)S(1)}, u32[]{:S(2)}) copy-start(bf16[128,768]{0,1:T(8,128)(2,1)S(1)} %copy.36) | copy-start | bytes 589828
  95.7 14.1 %copy-start.10 = (f32[1536]{0:T(1024)S(1)}, f32[1536]{0:T(1024)}, u32[]{:S(2)}) copy-start(f32[1536]{0:T(1024)} %get-tuple-element.26) | copy-start | bytes 18436
  95.7 14.1 %copy-start.9 = (f32[1536]{0:T(1024)S(1)}, f32[1536]{0:T(1024)}, u32[]{:S(2)}) copy-start(f32[1536]{0:T(1024)} %get-tuple-element.27) | copy-start | bytes 18436
  95.7 14.1 %copy-start.8 = (f32[1536]{0:T(1024)S(1)}, f32[1536]{0:T(1024)}, u32[]{:S(2)}) copy-start(f32[1536]{0:T(1024)} %get-tuple-element.28) | copy-start | bytes 18436
  95.7 14.1 %copy-start.7 = (f32[1536]{0:T(1024)S(1)}, f32[1536]{0:T(1024)}, u32[]{:S(2)}) copy-start(f32[1536]{0:T(1024)} %get-tuple-element.29) | copy-start | bytes 18436
  95.7 14.1 %copy-start.17 = (f32[1536]{0:T(1024)S(1)}, f32[1536]{0:T(1024)}, u32[]{:S(2)}) copy-start(f32[1536]{0:T(1024)} %get-tuple-element.32) | copy-start | bytes 18436
  95.7 14.2 %copy-start.16 = (f32[1536]{0:T(1024)S(1)}, f32[1536]{0:T(1024)}, u32[]{:S(2)}) copy-start(f32[1536]{0:T(1024)} %get-tuple-element.33) | copy-start | bytes 18436
  95.8 14.2 %copy-start.15 = (f32[1536]{0:T(1024)S(1)}, f32[1536]{0:T(1024)}, u32[]{:S(2)}) copy-start(f32[1536]{0:T(1024)} %get-tuple-element.34) | copy-start | bytes 18436
  95.8 14.2 %copy-start.14 = (f32[1536]{0:T(1024)S(1)}, f32[1536]{0:T(1024)}, u32[]{:S(2)}) copy-start(f32[1536]{0:T(1024)} %get-tuple-element.35) | copy-start | bytes 18436
  95.8 14.2 %copy-start.27 = (f32[1,1536]{1,0:T(1,128)S(1)}, f32[1,1536]{1,0:T(1,128)}, u32[]{:S(2)}) copy-start(f32[1,1536]{1,0:T(1,128)} %reshape.271) | copy-start | bytes 18436
  95.8 14.2 %copy-start.28 = (f32[1,1536]{1,0:T(1,128)S(1)}, f32[1,1536]{1,0:T(1,128)}, u32[]{:S(2)}) copy-start(f32[1,1536]{1,0:T(1,128)} %reshape.272) | copy-start | bytes 18436
  95.8 14.2 %copy-start.29 = (f32[1,1536]{1,0:T(1,128)S(1)}, f32[1,1536]{1,0:T(1,128)}, u32[]{:S(2)}) copy-start(f32[1,1536]{1,0:T(1,128)} %reshape.273) | copy-start | bytes 18436
  95.8 14.2 %copy-start.30 = (f32[1,1536]{1,0:T(1,128)S(1)}, f32[1,1536]{1,0:T(1,128)}, u32[]{:S(2)}) copy-start(f32[1,1536]{1,0:T(1,128)} %reshape.274) | copy-start | bytes 18436
  96.8 157.1 %all-to-all-start.1 = ((bf16[32,4,2304]{2,1,0:T(4,128)(2,1)}), bf16[32,4,2304]{2,1,0:T(4,128)(2,1)S(1)}, u32[]{:S(2)}, u32[]{:S(2)}) async-start(bf16[32,4,2304]{2,1,0:T(4,128)(2,1)} %all_to_all.25), calls=%async_computation.1 | async-start | bytes 1179648 | tf_op jit(solution)/shard_map/all_to_all | solution.py:119
  107.1 144.2 %all-reduce.66.cloned.1.call-start = ((), (), s32[]{:S(2)}) async-start(), calls=%async_computation.6 | async-start | bytes 393216 | tf_op jit(solution)/shard_map/psum | solution.py:123
  253.8 29.7 %all-to-all-start.2 = ((f32[32,1,4608]{2,1,0:T(1,128)}), f32[32,1,4608]{2,1,0:T(1,128)S(1)}, u32[]{:S(2)}, u32[]{:S(2)}) async-start(f32[32,1,4608]{2,1,0:T(1,128)} %all_to_all.30), calls=%async_computation.3 | async-start | bytes 1179648 | tf_op jit(solution)/shard_map/all_to_all | solution.py:146
  (25 other events, 198.5 us)
Sparse Core Ops, SparseCore 0:
  10.1 46.2 all-gather.3
  78.9 58.4 reduce-scatter.1
  140.4 110.8 all-reduce.65
where the time goes:
time: 342 us
  waiting for transfers between devices  184 us (54%)
  blocking collectives  48.8 us (14%)
  starting transfers between devices  33.8 us (10%)
  other arithmetic  28.4 us (8%)
  local copies, waits for them, and re-layouts  17.9 us (5%)
  between operations  14.9 us (4%)
  matrix products  14 us (4%)
    psum x1, waiting for transfers between devices, body(): kernel_f = lax.psum(kernel_part, 'fsdp')  113 us
    all_gather x1, blocking collectives, dp_allreduce_a2a(): return lax.all_gather(part, 'dp', axis=0, tiled=True).reshape(x.shape)  48.8 us
    reduce_scatter x1, waiting for transfers between devices, body(): lax.psum_scatter(jnp.einsum('rc,rd->cd', columns, mixed_grad, preferred_e...  26.3 us
    all_to_all x1, waiting for transfers between devices, body(): lax.all_to_all(outgoing, 'dp', split_axis=0, concat_axis=0, tiled=True)  17.5 us
    all_to_all x1, waiting for transfers between devices, dp_allreduce_a2a(): got = lax.all_to_all(flat, 'dp', split_axis=0, concat_axis=0, tiled=True)  17 us
    reduce_sum x4, other arithmetic, finish(): kernel[offset] * padded[offset:offset + length] * matching[:, None]  14.9 us
    all_to_all x1, starting transfers between devices, body(): lax.all_to_all(outgoing, 'dp', split_axis=0, concat_axis=0, tiled=True)  13.2 us
    all_to_all x1, starting transfers between devices, body(): lax.all_to_all(returning, 'dp', split_axis=0, concat_axis=0, tiled=True)  10.3 us
  transfers between devices with their start and end apart: 6, of which 5 were waited for; matrix products, arithmetic and copies ran while one was open for 9% of the time, Pallas kernels for 0%

commit v1 on v0

--- a/solution.py
+++ b/solution.py
@@ -5,6 +5,12 @@
 
 HEADS = 8
 HEAD_DIM = 96
+
+
+def gather_and_add(shard, axis):
+    blocks = lax.all_gather(shard, axis, axis=0, tiled=False)
+    acc = blocks.sum(axis=0)
+    return acc
 
 
 def split_heads(frames):
@@ -120,7 +126,7 @@
     source_index = jnp.where(present, send_rows, row_count)
     projected_grad = jnp.zeros_like(projected).at[source_index].set(arrived, mode="drop")
     scale_factor = (row_count * lax.axis_size("dp") * lax.axis_size("fsdp")) ** (-0.5)
-    kernel_f = lax.psum(kernel_part, "fsdp")
+    kernel_f = gather_and_add(kernel_part, "fsdp")
     both = dp_allreduce_a2a(
         jnp.concatenate([weight_share, kernel_f, jnp.zeros((17, 1536), jnp.float32)], axis=0)
     )

time: 342 us -> 278 us (0.81)
  the two profiles are of different devices: /device:TPU:24 before, /device:TPU:8 now
where the time goes in v1:
time: 278 us; the launch traced here: 277 us
  waiting for transfers between devices  125 us (45%)
  blocking collectives  48.6 us (17%)
  starting transfers between devices  33.7 us (12%)
  other arithmetic  29.2 us (11%)
  between operations  15 us (5%)
  matrix products  13.2 us (5%)
  local copies, waits for them, and re-layouts  12.2 us (4%)
    all_gather x1, blocking collectives, dp_allreduce_a2a(): return lax.all_gather(part, 'dp', axis=0, tiled=True).reshape(x.shape)  48.6 us
    all_gather x1, waiting for transfers between devices, gather_and_add(): blocks = lax.all_gather(shard, axis, axis=0, tiled=False)  47.1 us
    reduce_scatter x1, waiting for transfers between devices, body(): lax.psum_scatter(jnp.einsum('rc,rd->cd', columns, mixed_grad, preferred_e...  34.1 us
    all_to_all x1, waiting for transfers between devices, body(): lax.all_to_all(outgoing, 'dp', split_axis=0, concat_axis=0, tiled=True)  17.4 us
    all_to_all x1, waiting for transfers between devices, dp_allreduce_a2a(): got = lax.all_to_all(flat, 'dp', split_axis=0, concat_axis=0, tiled=True)  16.8 us
    reduce_sum x4, other arithmetic, finish(): kernel[offset] * padded[offset:offset + length] * matching[:, None]  14.6 us
    all_to_all x1, starting transfers between devices, body(): lax.all_to_all(outgoing, 'dp', split_axis=0, concat_axis=0, tiled=True)  13.2 us
    all_to_all x1, starting transfers between devices, body(): lax.all_to_all(returning, 'dp', split_axis=0, concat_axis=0, tiled=True)  10.2 us
  transfers between devices with their start and end apart: 6, of which 5 were waited for; matrix products, arithmetic and copies ran while one was open for 9% of the time, Pallas kernels for 0%

profile of v1, /device:TPU:8, one launch (start us, length us, event | category | flops | bytes accessed | tf_op | source)
XLA Modules:
  0.0 277.1 jit_solution(15437864007302919887)
XLA Ops:
  7.9 1.2 compare_select_fusion.1
  9.2 1.0 gather_fusion
  10.4 1.0 all_to_all.22
  11.3 13.2 %all-to-all-start = ((bf16[32,4,2304]{2,1,0:T(4,128)(2,1)}), bf16[32,4,2304]{2,1,0:T(4,128)(2,1)S(1)}, u32[]{:S(2)}, u32[]{:S(2)}) async-start(bf16[32,4,2304]{2,1,0:T(4,128)(2,1)} %all_to_all.22), calls=%async_computation | async-start | bytes 1179648 | tf_op jit(solution)/shard_map/all_to_all | solution.py:90
  26.1 17.4 %all-to-all-done = bf16[32,4,2304]{2,1,0:T(4,128)(2,1)S(1)} async-done(((bf16[32,4,2304]{2,1,0:T(4,128)(2,1)}), bf16[32,4,2304]{2,1,0:T(4,128)(2,1)S(1)}, u32[]{:S(2)}, u32[]{:S(2)}) %all-to-all-start) | async-done | bytes 589856 | tf_op jit(solution)/shard_map/all_to_all | solution.py:90
  43.6 1.0 gather_fusion.1
  45.3 1.2 fusion.40
  47.6 9.0 %all-gather.7.cloned.1.call-done = bf16[768,1536]{1,0:T(8,128)(2,1)} async-done(((bf16[48,1536]{1,0:T(8,128)(2,1)}), bf16[768,1536]{1,0:T(8,128)(2,1)}) %all-gather.7.cloned.1.call-update) | async-done | bytes 2359312 | tf_op jit(solution)/shard_map/all_gather | solution.py:98
  56.6 2.2 fusion.2
  58.8 7.8 %multiply_reduce_fusion.31 = (f32[1536]{0:T(1024)}, f32[1536]{0:T(1024)}, f32[1536]{0:T(1024)}, f32[1536]{0:T(1024)}, f32[1536]{0:T(1024)}, /*index=5*/f32[1536]...) fusion(f32[128,1536]{1,0:T(8,128)S(1)} %fusion.2, ...), kind=kLoop, calls=%fused_computation.99 | loop fusion | flops 25152000 | bytes 3013632 | tf_op jit(solution)/shard_map/transpose(jvp())/reduce_sum | solution.py:80
  66.6 2.2 multiply_reduce_fusion.16
  70.8 2.6 multiply_reduce_fusion.4
  73.5 2.6 pad_add_fusion
  76.9 2.2 convolution_convert_fusion
  79.6 2.0 multiply_reduce_fusion.22
  82.0 1.0 add_bitcast_fusion
  83.0 2.5 convolution_convert_fusion.5
  85.7 1.3 convolution_convert_fusion.2
  87.4 1.6 convolution_convert_fusion.3
  89.2 1.6 convolution_convert_fusion.4
  90.9 1.8 scatter_custom_fusion
  92.7 1.0 all_to_all.25
  93.6 10.2 %all-to-all-start.1 = ((bf16[32,4,2304]{2,1,0:T(4,128)(2,1)}), bf16[32,4,2304]{2,1,0:T(4,128)(2,1)S(1)}, u32[]{:S(2)}, u32[]{:S(2)}) async-start(bf16[32,4,2304]{2,1,0:T(4,128)(2,1)} %all_to_all.25), calls=%async_computation.1 | async-start | bytes 1179648 | tf_op jit(solution)/shard_map/all_to_all | solution.py:125
  103.9 34.1 %reduce-scatter.2.cloned.1.call-done = bf16[48,1536]{1,0:T(8,128)(2,1)} async-done(((bf16[768,1536]{1,0:T(8,128)(2,1)}), bf16[48,1536]{1,0:T(8,128)(2,1)}) %reduce-scatter.2.cloned.1.call-update) | async-done | bytes 147472 | tf_op jit(solution)/shard_map/reduce_scatter | solution.py:107
  138.0 0.9 convert_element_type.212
  138.9 47.1 %all-gather.9.cloned.1.call-done = f32[16,31,1536]{2,1,0:T(8,128)} async-done(((f32[1,31,1536]{2,1,0:T(8,128)}), f32[16,31,1536]{2,1,0:T(8,128)}) %all-gather.9.cloned.1.call-update) | async-done | bytes 3047440 | tf_op jit(solution)/shard_map/all_gather | solution.py:11
  186.1 2.1 reduce_sum.364
  188.3 1.5 all_to_all.30
  189.8 10.2 %all-to-all-start.2 = ((f32[32,1,4608]{2,1,0:T(1,128)}), f32[32,1,4608]{2,1,0:T(1,128)S(1)}, u32[]{:S(2)}, u32[]{:S(2)}) async-start(f32[32,1,4608]{2,1,0:T(1,128)} %all_to_all.30), calls=%async_computation.3 | async-start | bytes 1179648 | tf_op jit(solution)/shard_map/all_to_all | solution.py:152
  200.1 2.4 scatter_custom_fusion.1
  202.5 16.8 %all-to-all-done.2 = f32[32,1,4608]{2,1,0:T(1,128)S(1)} async-done(((f32[32,1,4608]{2,1,0:T(1,128)}), f32[32,1,4608]{2,1,0:T(1,128)S(1)}, u32[]{:S(2)}, u32[]{:S(2)}) %all-to-all-start.2) | async-done | bytes 589856 | tf_op jit(solution)/shard_map/all_to_all | solution.py:152
  219.7 48.6 %all-gather.3 = f32[32,1,4608]{2,1,0:T(1,128)S(1)} all-gather(f32[1,1,4608]{2,1,0:T(1,128)S(1)} %reshape.351), channel_id=3, replica_groups=mesh['dp'=32,'fsdp'=16] {'dp'}, dimensions={0}, use_global_device_ids=true | all-gather | bytes 608256 | tf_op jit(solution)/shard_map/all_gather | solution.py:154
  (173 shorter events, 11.1 us)
Async XLA Ops:
  7.2 49.4 %all-gather.7.cloned.1.call-start = ((), (), s32[]{:S(2)}) async-start(), calls=%async_computation.4 | async-start | bytes 2506752 | tf_op jit(solution)/shard_map/all_gather | solution.py:98
  10.2 14.4 %copy-start.4 = (f32[31,1536]{1,0:T(8,128)S(1)}, f32[31,1536]{1,0:T(8,128)}, u32[]{:S(2)}) copy-start(f32[31,1536]{1,0:T(8,128)} %param.11) | copy-start | bytes 571396
  10.2 14.6 %copy-start.46 = (s32[128]{0:T(128)S(1)}, s32[128]{0:T(128)}, u32[]{:S(2)}) copy-start(s32[128]{0:T(128)} %param.14) | copy-start | bytes 1540
  10.2 15.5 %copy-start.44 = (s32[128]{0:T(128)S(1)}, s32[128]{0:T(128)}, u32[]{:S(2)}) copy-start(s32[128]{0:T(128)} %param.15) | copy-start | bytes 1540
  11.3 32.2 %all-to-all-start = ((bf16[32,4,2304]{2,1,0:T(4,128)(2,1)}), bf16[32,4,2304]{2,1,0:T(4,128)(2,1)S(1)}, u32[]{:S(2)}, u32[]{:S(2)}) async-start(bf16[32,4,2304]{2,1,0:T(4,128)(2,1)} %all_to_all.22), calls=%async_computation | async-start | bytes 1179648 | tf_op jit(solution)/shard_map/all_to_all | solution.py:90
  24.5 113.5 %reduce-scatter.2.cloned.1.call-start = ((), (), s32[]{:S(2)}) async-start(), calls=%async_computation.5 | async-start | bytes 2506752 | tf_op jit(solution)/shard_map/reduce_scatter | solution.py:107
  25.9 43.4 %copy-start.38 = (f32[128]{0:T(128)}, f32[128]{0:T(128)S(1)}, u32[]{:S(2)}) copy-start(f32[128]{0:T(128)S(1)} %get-tuple-element.120) | copy-start | bytes 1540
  25.9 43.4 %copy-start.40 = (f32[128]{0:T(128)}, f32[128]{0:T(128)S(1)}, u32[]{:S(2)}) copy-start(f32[128]{0:T(128)S(1)} %get-tuple-element.121) | copy-start | bytes 1540
  25.9 43.4 %copy-start.42 = (f32[128]{0:T(128)}, f32[128]{0:T(128)S(1)}, u32[]{:S(2)}) copy-start(f32[128]{0:T(128)S(1)} %get-tuple-element.122) | copy-start | bytes 1540
  25.9 44.2 %copy-start.26 = (f32[128]{0:T(128)}, f32[128]{0:T(128)S(1)}, u32[]{:S(2)}) copy-start(f32[128]{0:T(128)S(1)} %get-tuple-element.114) | copy-start | bytes 1540
  25.9 44.2 %copy-start.28 = (f32[128]{0:T(128)}, f32[128]{0:T(128)S(1)}, u32[]{:S(2)}) copy-start(f32[128]{0:T(128)S(1)} %get-tuple-element.115) | copy-start | bytes 1540
  25.9 44.2 %copy-start.30 = (f32[128]{0:T(128)}, f32[128]{0:T(128)S(1)}, u32[]{:S(2)}) copy-start(f32[128]{0:T(128)S(1)} %get-tuple-element.116) | copy-start | bytes 1540
  25.9 44.2 %copy-start.32 = (f32[128]{0:T(128)}, f32[128]{0:T(128)S(1)}, u32[]{:S(2)}) copy-start(f32[128]{0:T(128)S(1)} %get-tuple-element.117) | copy-start | bytes 1540
  25.9 44.2 %copy-start.34 = (f32[128]{0:T(128)}, f32[128]{0:T(128)S(1)}, u32[]{:S(2)}) copy-start(f32[128]{0:T(128)S(1)} %get-tuple-element.118) | copy-start | bytes 1540
  26.0 44.2 %copy-start.36 = (f32[128]{0:T(128)}, f32[128]{0:T(128)S(1)}, u32[]{:S(2)}) copy-start(f32[128]{0:T(128)S(1)} %get-tuple-element.119) | copy-start | bytes 1540
  26.1 20.4 %copy-start.25 = (pred[128,128]{0,1:T(8,128)(4,1)}, pred[128,128]{0,1:T(8,128)(4,1)S(1)}, u32[]{:S(2)}) copy-start(pred[128,128]{0,1:T(8,128)(4,1)S(1)} %broadcast_compare_fusion) | copy-start | bytes 49156
  45.1 11.5 %copy-start.2 = (bf16[128,768]{0,1:T(8,128)(2,1)}, bf16[128,768]{0,1:T(8,128)(2,1)S(1)}, u32[]{:S(2)}) copy-start(bf16[128,768]{0,1:T(8,128)(2,1)S(1)} %copy.35) | copy-start | bytes 589828
  47.6 11.2 %copy-start.1 = (bf16[128,1536]{1,0:T(8,128)(2,1)S(1)}, bf16[128,1536]{1,0:T(8,128)(2,1)}, u32[]{:S(2)}) copy-start(bf16[128,1536]{1,0:T(8,128)(2,1)} %param.12) | copy-start | bytes 1179652
  76.8 2.6 copy-start.27
  79.1 2.6 copy-start.8
  79.1 2.7 copy-start.7
  79.1 2.7 copy-start.6
  79.1 2.7 copy-start.5
  79.1 2.7 copy-start.24
  79.2 2.8 copy-start.23
  79.2 2.8 copy-start.22
  79.2 2.8 %copy-start.21 = (f32[1536]{0:T(1024)S(1)}, f32[1536]{0:T(1024)}, u32[]{:S(2)}) copy-start(f32[1536]{0:T(1024)} %get-tuple-element.35) | copy-start | bytes 18436
  79.2 106.9 %all-gather.9.cloned.1.call-start = ((), (), s32[]{:S(2)}) async-start(), calls=%async_computation.6 | async-start | bytes 3342336 | tf_op jit(solution)/shard_map/all_gather | solution.py:11
  81.5 4.2 %copy-start.3 = (bf16[128,768]{0,1:T(8,128)(2,1)S(1)}, bf16[128,768]{0,1:T(8,128)(2,1)}, u32[]{:S(2)}) copy-start(bf16[128,768]{0,1:T(8,128)(2,1)} %copy-done.2) | copy-start | bytes 589828
  81.5 4.2 %copy-start.48 = (f32[8,128]{1,0:T(8,128)S(1)}, f32[8,128]{1,0:T(8,128)}, u32[]{:S(2)}) copy-start(f32[8,128]{1,0:T(8,128)} %copy-done.47) | copy-start | bytes 12292
  93.6 96.2 %all-to-all-start.1 = ((bf16[32,4,2304]{2,1,0:T(4,128)(2,1)}), bf16[32,4,2304]{2,1,0:T(4,128)(2,1)S(1)}, u32[]{:S(2)}, u32[]{:S(2)}) async-start(bf16[32,4,2304]{2,1,0:T(4,128)(2,1)} %all_to_all.25), calls=%async_computation.1 | async-start | bytes 1179648 | tf_op jit(solution)/shard_map/all_to_all | solution.py:125
  189.8 29.6 %all-to-all-start.2 = ((f32[32,1,4608]{2,1,0:T(1,128)}), f32[32,1,4608]{2,1,0:T(1,128)S(1)}, u32[]{:S(2)}, u32[]{:S(2)}) async-start(f32[32,1,4608]{2,1,0:T(1,128)} %all_to_all.30), calls=%async_computation.3 | async-start | bytes 1179648 | tf_op jit(solution)/shard_map/all_to_all | solution.py:152
  (23 other events, 55.6 us)
Sparse Core Ops, SparseCore 0:
  10.1 46.4 all-gather.6
  79.3 58.6 reduce-scatter.1
  140.7 45.3 all-gather.8
